TPU v7x, 32 devices: a whole 2x2x4 slice. The times are simulated.
32 devices in a mesh: dp: 8 (over y, x, core), tensor: 4 (over z).
Axes of the slice: x: 2, y: 2, z: 4, core: 2. Of those that a mesh axis runs over, the one named last changes fastest.
Arguments:
- tokens: bfloat16 [16384, 768], P(('dp', 'tensor')), may hold values from -6 to 6
- out_grad: bfloat16 [16384, 768], P(('dp', 'tensor')), may hold values from -6 to 6
- lengths: int32 [32], P('dp'), may hold values from 20 to 512, as said below
- qkv_weight: bfloat16 [3, 768, 768], P(None, None, 'tensor'), may hold values from -0.21875 to 0.21875
- qkv_bias: bfloat16 [2, 768], P(None, 'tensor'), may hold values from -3 to 3
- out_weight: bfloat16 [768, 768], P('tensor'), may hold values from -1.75 to 1.75
- out_bias: float32 [768], replicated, may hold values from -3 to 3
- norm1_gain: float32 [768], replicated, may hold values from 0.5 to 1.5
- norm1_shift: float32 [768], replicated, may hold values from -3 to 3
- up_weight: bfloat16 [768, 3072], P(None, 'tensor'), may hold values from -0.21875 to 0.21875
- up_bias: bfloat16 [3072], P('tensor'), may hold values from -3 to 3
- down_weight: bfloat16 [3072, 768], P('tensor'), may hold values from -0.109375 to 0.109375
- down_bias: float32 [768], replicated, may hold values from -3 to 3
- norm2_gain: float32 [768], replicated, may hold values from 0.5 to 1.5
- norm2_shift: float32 [768], replicated, may hold values from -3 to 3
Outputs:
- layer_out: bfloat16 [16384, 768], P(('dp', 'tensor'))
- input_grad: bfloat16 [16384, 768], P(('dp', 'tensor'))
- grad_qkv_weight: float32 [3, 768, 768], P(None, None, 'tensor')
- grad_qkv_bias: float32 [2, 768], P(None, 'tensor')
- grad_out_weight: float32 [768, 768], P('tensor')
- grad_out_bias: float32 [768], replicated
- grad_norm1_gain: float32 [768], replicated
- grad_norm1_shift: float32 [768], replicated
- grad_up_weight: float32 [768, 3072], P(None, 'tensor')
- grad_up_bias: float32 [3072], P('tensor')
- grad_down_weight: float32 [3072, 768], P('tensor')
- grad_down_bias: float32 [768], replicated
- grad_norm2_gain: float32 [768], replicated
- grad_norm2_shift: float32 [768], replicated
Inputs may be any that keep to these rules, and one draw needn't show every extreme that they name: Keys at positions lengths[p] and beyond of passage p are padding; some passage has exactly 512 and some exactly 20.
All inputs are finite; a program needn't handle non-finite values.
Results may differ from a plain program's by a relative error of at most 0.02.
Values may be sent and summed in bfloat16 or wider, within the bound.
No kernel may reach another device: no remote copies, remote signals or barrier semaphores. Data moves between devices by JAX's collectives and lax.ppermute only.
A program may use at most 128 MiB of HBM per device.

v0:
```python
import jax
import jax.numpy as jnp
from jax import lax
from jax.sharding import PartitionSpec as P

HD = 64
LEN = 512
EPS = 1e-12
NEG = -1e30


def layer_norm(values, gain_vec, shift_vec):
    center = values - jnp.mean(values, axis=-1, keepdims=True)
    spread = jnp.mean(center * center, axis=-1, keepdims=True)
    return center * lax.rsqrt(spread + EPS) * gain_vec + shift_vec


def gelu_exact(values):
    return jax.nn.gelu(values, approximate=False)


def contract(left, right, left_dim, right_dim):
    return lax.dot_general(
        left, right, (((left_dim,), (right_dim,)), ((), ())), preferred_element_type=jnp.float32
    )


def attend_forward(queries, key_rows, value_rows, usable, factor):
    scores = (
        jnp.einsum("pqhe,pkhe->phqk", queries, key_rows, preferred_element_type=jnp.float32)
        * factor
    )
    scores = jnp.where(usable[:, None, None, :], scores, NEG)
    log_total = jax.nn.logsumexp(scores, axis=-1, keepdims=True)
    attn_probs = jnp.exp(scores - log_total)
    context = jnp.einsum(
        "phqk,pkhe->pqhe",
        attn_probs.astype(jnp.bfloat16),
        value_rows,
        preferred_element_type=jnp.float32,
    )
    return (context, attn_probs)


def attend_backward(queries, key_rows, value_rows, attn_probs, context_grad, factor):
    prob_grad = jnp.einsum(
        "pqhe,pkhe->phqk", context_grad, value_rows, preferred_element_type=jnp.float32
    )
    row_dot = jnp.sum(prob_grad * attn_probs, axis=-1, keepdims=True)
    score_grad = (attn_probs * (prob_grad - row_dot)).astype(jnp.bfloat16)
    query_grad = (
        jnp.einsum("phqk,pkhe->pqhe", score_grad, key_rows, preferred_element_type=jnp.float32)
        * factor
    )
    key_grad = (
        jnp.einsum("phqk,pqhe->pkhe", score_grad, queries, preferred_element_type=jnp.float32)
        * factor
    )
    value_grad = jnp.einsum(
        "phqk,pqhe->pkhe",
        attn_probs.astype(jnp.bfloat16),
        context_grad,
        preferred_element_type=jnp.float32,
    )
    return (query_grad, key_grad, value_grad)


def dp_pow2(values, dp_size):
    steps = dp_size.bit_length() - 1
    return dp_size == 1 << steps and values.shape[0] % dp_size == 0


def dp_halve(values, dp_size, sum_dtype=None):
    steps = dp_size.bit_length() - 1
    index = lax.axis_index("dp")
    link = values.dtype
    kept = values if sum_dtype is None else values.astype(sum_dtype)
    for step in range(steps):
        bit = index >> step & 1
        half = kept.shape[0] // 2
        keep = lax.dynamic_slice_in_dim(kept, bit * half, half)
        give = lax.dynamic_slice_in_dim(kept, (1 - bit) * half, half).astype(link)
        got = lax.ppermute(give, "dp", [(i, i ^ 1 << step) for i in range(dp_size)])
        kept = keep + got.astype(kept.dtype)
    return kept


def bit_reversed(count):
    steps = count.bit_length() - 1
    return [int(format(i, f"0{steps}b")[::-1], 2) if steps else 0 for i in range(count)]


def dp_double(kept, dp_size):
    steps = dp_size.bit_length() - 1
    index = lax.axis_index("dp")
    for step in reversed(range(steps)):
        bit = index >> step & 1
        got = lax.ppermute(kept, "dp", [(i, i ^ 1 << step) for i in range(dp_size)])
        kept = jnp.concatenate([jnp.where(bit == 0, kept, got), jnp.where(bit == 0, got, kept)])
    return kept


def make_per_device(dp_size):

    def per_device(
        tokens,
        out_grad,
        lengths,
        qkv_weight,
        qkv_bias,
        out_weight,
        out_bias,
        norm1_gain,
        norm1_shift,
        up_weight,
        up_bias,
        down_weight,
        down_bias,
        norm2_gain,
        norm2_shift,
    ):
        rows, width = tokens.shape
        shard = qkv_weight.shape[2]
        groups = width // shard
        passages = rows // LEN
        heads = width // HD
        factor = HD ** (-0.5)
        packed_w = jnp.concatenate(
            [qkv_weight.reshape(3 * width, shard), out_weight.T, qkv_bias], axis=0
        )
        w_rows = packed_w.shape[0]
        half_rows = -(-w_rows // 16) * 8
        packed_w = jnp.pad(packed_w, ((0, 2 * half_rows - w_rows), (0, 0)))
        dp_index = lax.axis_index("dp")
        parity = dp_index % 2
        mine = lax.dynamic_slice_in_dim(packed_w, parity * half_rows, half_rows)
        mine = lax.all_gather(mine, "tensor", axis=0, tiled=False)
        other = lax.ppermute(mine, "dp", [(i, i ^ 1) for i in range(dp_size)])
        first = jnp.where(parity == 0, mine, other)
        second = jnp.where(parity == 0, other, mine)
        weights_all = jnp.concatenate([first, second], axis=1)[:, :w_rows]
        qkv_blocks = weights_all[:, : 3 * width].reshape(groups, 3, width, shard)
        proj_blocks = weights_all[:, 3 * width : 4 * width]
        bias_full = weights_all[:, 4 * width :].transpose(1, 0, 2).reshape(2, width)
        tensor_index = lax.axis_index("tensor")
        own_lengths = lax.dynamic_slice_in_dim(lengths, tensor_index * passages, passages)
        usable = jnp.arange(LEN, dtype=jnp.int32)[None, :] < own_lengths[:, None]
        own_tokens = tokens.astype(jnp.float32)
        projected = jnp.einsum(
            "rd,gtdj->trgj", tokens, qkv_blocks, preferred_element_type=jnp.float32
        ).reshape(3, rows, width)
        four_dims = (passages, LEN, heads, HD)
        queries = (projected[0] + bias_full[0]).astype(jnp.bfloat16).reshape(four_dims)
        key_rows = projected[1].astype(jnp.bfloat16).reshape(four_dims)
        value_rows = (projected[2] + bias_full[1]).astype(jnp.bfloat16).reshape(four_dims)
        context, attn_probs = attend_forward(queries, key_rows, value_rows, usable, factor)
        context_low = context.reshape(rows, width).astype(jnp.bfloat16)
        attn_out = jnp.einsum(
            "rgj,gcj->rc",
            context_low.reshape(rows, groups, shard),
            proj_blocks,
            preferred_element_type=jnp.float32,
        )
        middle, norm1_back = jax.vjp(
            layer_norm, own_tokens + attn_out + out_bias, norm1_gain, norm1_shift
        )
        middle_low = middle.astype(jnp.bfloat16)
        ffn_rows = lax.all_gather(middle_low, "tensor", axis=0, tiled=True)
        pre_act = jnp.dot(ffn_rows, up_weight, preferred_element_type=jnp.float32) + up_bias
        activated, gelu_back = jax.vjp(gelu_exact, pre_act)
        hidden = activated.astype(jnp.bfloat16)
        ffn_out = lax.psum_scatter(
            jnp.dot(hidden, down_weight, preferred_element_type=jnp.float32).astype(jnp.bfloat16),
            "tensor",
            scatter_dimension=0,
            tiled=True,
        ).astype(jnp.float32)
        layer_out, norm2_back = jax.vjp(
            layer_norm, middle + ffn_out + down_bias, norm2_gain, norm2_shift
        )
        second_grad, grad_norm2_gain, grad_norm2_shift = norm2_back(out_grad.astype(jnp.float32))
        branch_grad = second_grad.astype(jnp.bfloat16)
        grad_down_bias = jnp.sum(branch_grad, axis=0, dtype=jnp.float32)
        branch_rows = lax.all_gather(branch_grad, "tensor", axis=0, tiled=True)
        hidden_grad = contract(branch_rows, down_weight, 1, 1)
        grad_down_weight = contract(hidden, branch_rows, 0, 0)
        pre_grad = gelu_back(hidden_grad)[0].astype(jnp.bfloat16)
        grad_up_bias = jnp.sum(pre_grad, axis=0, dtype=jnp.float32)
        grad_up_weight = contract(ffn_rows, pre_grad, 0, 0)
        ffn_grads = (grad_up_weight, grad_down_weight)
        halved = all((dp_pow2(g, dp_size) for g in ffn_grads))
        if halved:
            ffn_grads = tuple((dp_halve(g, dp_size) for g in ffn_grads))
        else:
            ffn_grads = lax.psum(ffn_grads, "dp")
        middle_part = lax.psum_scatter(
            contract(pre_grad, up_weight, 1, 1).astype(jnp.bfloat16),
            "tensor",
            scatter_dimension=0,
            tiled=True,
        ).astype(jnp.float32)
        norm1_in, ffn_grads = lax.optimization_barrier((second_grad + middle_part, ffn_grads))
        first_grad, grad_norm1_gain, grad_norm1_shift = norm1_back(norm1_in)
        attn_grad = first_grad.astype(jnp.bfloat16)
        grad_out_bias = jnp.sum(attn_grad, axis=0, dtype=jnp.float32)
        context_grad = (
            jnp.einsum("rc,gcj->rgj", attn_grad, proj_blocks, preferred_element_type=jnp.float32)
            .astype(jnp.bfloat16)
            .reshape(four_dims)
        )
        early = contract(attn_grad, context_low, 0, 0)
        early_halved = dp_pow2(early, dp_size)
        if early_halved:
            early = dp_halve(early.astype(jnp.bfloat16), dp_size, jnp.float32)
        else:
            early = lax.psum_scatter(early, "dp", scatter_dimension=0, tiled=True)
        query_grad, key_grad, value_grad = attend_backward(
            queries, key_rows, value_rows, attn_probs, context_grad, factor
        )
        proj_grad = (
            jnp.stack([query_grad, key_grad, value_grad])
            .reshape(3, rows, width)
            .astype(jnp.bfloat16)
        )
        grad_bias_full = jnp.sum(proj_grad[0::2], axis=1, dtype=jnp.float32)
        grad_qkv_full = jnp.einsum(
            "rd,tre->tde", tokens, proj_grad, preferred_element_type=jnp.float32
        )
        input_part = jnp.einsum(
            "trgj,gtdj->rd",
            proj_grad.reshape(3, rows, groups, shard),
            qkv_blocks,
            preferred_element_type=jnp.float32,
        )
        input_grad = (first_grad + input_part).astype(jnp.bfloat16)
        small = jnp.stack(
            [
                grad_out_bias,
                grad_norm1_gain,
                grad_norm1_shift,
                grad_down_bias,
                grad_norm2_gain,
                grad_norm2_shift,
            ]
        )
        n_small = small.shape[0]
        small_rep = jnp.tile(small.reshape(n_small, groups, shard), (1, 1, groups)).reshape(
            n_small * groups, width
        )
        up_parts = grad_up_bias.shape[0] // shard
        own_group = (jnp.arange(width) // shard == tensor_index)[None, :]
        up_rep = jnp.where(
            own_group, jnp.tile(grad_up_bias.reshape(up_parts, shard), (1, groups)), 0.0
        )
        tail = jnp.concatenate([grad_bias_full, small_rep, up_rep], axis=0)
        tail_rows = tail.shape[0]
        tail = jnp.pad(tail, ((0, -(-tail_rows // 8) * 8 - tail_rows), (0, 0)))
        late = lax.psum_scatter(
            grad_qkv_full.reshape(3 * width, width).astype(jnp.bfloat16),
            "dp",
            scatter_dimension=0,
            tiled=True,
        ).astype(jnp.float32)
        joined = jnp.concatenate([late, early, tail], axis=0)
        joined = lax.psum_scatter(
            joined.reshape(joined.shape[0], groups, shard).transpose(1, 0, 2),
            "tensor",
            scatter_dimension=0,
            tiled=True,
        )[0]
        if halved:
            ffn_grads = tuple(
                (dp_double(g.astype(jnp.bfloat16), dp_size).astype(jnp.float32) for g in ffn_grads)
            )
            joined, ffn_grads = lax.optimization_barrier((joined, ffn_grads))
        grad_up_weight, grad_down_weight = ffn_grads
        late_rows = late.shape[0]
        early_rows = early.shape[0]
        joined = lax.all_gather(joined, "dp", axis=0, tiled=False)
        early = joined[:, late_rows : late_rows + early_rows]
        if early_halved:
            order = bit_reversed(dp_size)
            place = [order.index(b) for b in range(dp_size)]
            early = jnp.concatenate([early[p] for p in place], axis=0)
        pieces = [
            joined[:, :late_rows].reshape(-1, shard),
            early.reshape(-1, shard),
            jnp.sum(joined[:, late_rows + early_rows :], axis=0),
        ]
        grad_qkv_weight = pieces[0].reshape(3, width, shard)
        grad_out_weight = pieces[1].T
        tail = pieces[2]
        grad_qkv_bias = tail[:2]
        small_sum = tail[2 : 2 + n_small * groups].reshape(n_small, width)
        grad_up_bias = tail[2 + n_small * groups : 2 + n_small * groups + up_parts].reshape(-1)
        (
            grad_out_bias,
            grad_norm1_gain,
            grad_norm1_shift,
            grad_down_bias,
            grad_norm2_gain,
            grad_norm2_shift,
        ) = [small_sum[i] for i in range(n_small)]
        return (
            layer_out.astype(jnp.bfloat16),
            input_grad,
            grad_qkv_weight,
            grad_qkv_bias,
            grad_out_weight,
            grad_out_bias,
            grad_norm1_gain,
            grad_norm1_shift,
            grad_up_weight,
            grad_up_bias,
            grad_down_weight,
            grad_down_bias,
            grad_norm2_gain,
            grad_norm2_shift,
        )

    return per_device


def solution(mesh):
    placed = (
        P(("dp", "tensor"), None),
        P(("dp", "tensor"), None),
        P("dp"),
        P(None, None, "tensor"),
        P(None, "tensor"),
        P("tensor", None),
        P(),
        P(),
        P(),
        P(None, "tensor"),
        P("tensor"),
        P("tensor", None),
        P(),
        P(),
        P(),
    )
    return jax.shard_map(
        make_per_device(mesh.shape["dp"]),
        mesh=mesh,
        in_specs=placed,
        out_specs=(
            P(("dp", "tensor"), None),
            P(("dp", "tensor"), None),
            P(None, None, "tensor"),
            P(None, "tensor"),
            P("tensor", None),
            P(),
            P(),
            P(),
            P(None, "tensor"),
            P("tensor"),
            P("tensor", None),
            P(),
            P(),
            P(),
        ),
        check_vma=False,
    )
```

profile of v0, /device:TPU:0, one launch (start us, length us, event | category | flops | bytes accessed | tf_op | source)
XLA Modules:
  0.0 587.0 jit_solution(9950485908794336362)
XLA Ops:
  11.3 56.9 %all-gather.13.cloned.1.call-done = bf16[4,1544,192]{1,2,0:T(8,128)(2,1)} async-done(((bf16[1,1544,192]{1,2,0:T(8,128)(2,1)}), bf16[4,1544,192]{1,2,0:T(8,128)(2,1)}) %all-gather.13.cloned.1.call-update) | async-done | bytes 2371600 | tf_op jit(solution)/shard_map/all_gather | solution.py:137
  83.1 5.0 fusion
  92.7 10.1 %fusion.1 = bf16[12,512,512]{1,2,0:T(8,128)(2,1)} fusion(f32[12,512,512]{1,2,0:T(8,128)} %copy-done.2, f32[12,512]{1,0:T(8,128)S(1)} %log_add_fusion, pred[512]{0:T(512)(128)(4,1)S(1)} %iota_compare_fusion.1), kind=kLoop, calls=%fused_computation.7 | loop fusion | flops 12582912 | bytes 18899456 | tf_op jit(solution)/shard_map/convert_element_type | solution.py:38
  102.8 4.1 convolution_convert_fusion.5
  113.8 61.0 %all-gather.9.cloned.1.call-done = bf16[2048,768]{1,0:T(8,128)(2,1)} async-done(((bf16[512,768]{1,0:T(8,128)(2,1)}), bf16[2048,768]{1,0:T(8,128)(2,1)}) %all-gather.9.cloned.1.call-update) | async-done | bytes 3145744 | tf_op jit(solution)/shard_map/all_gather | solution.py:168
  174.8 18.5 %multiply_convert_fusion.1 = (bf16[2048,768]{1,0:T(8,128)(2,1)S(1)}, f32[2048,768]{1,0:T(8,128)}, f32[2048,768]{1,0:T(8,128)}) fusion(f32[768]{0:T(1024)} %convert_element_type.191, bf16[2048,768]{1,0:T(8,128)(2,1)} %all-gather.9.cloned.1.call-done, bf16[768,768]{1,0:T(8,128)(2,1)S(1)} %copy-done), kind=kOutput, calls=%fused_computation.11 | convolution fusion | flops 2519728128 | bytes 20057088 | tf_op jit(solution)/shard_map/dot_general | solution.py:169
  198.9 59.1 %reduce-scatter.5.cloned.1.call-done = bf16[512,768]{1,0:T(8,128)(2,1)} async-done(((bf16[2048,768]{1,0:T(8,128)(2,1)}), bf16[512,768]{1,0:T(8,128)(2,1)}) %reduce-scatter.5.cloned.1.call-update) | async-done | bytes 786448 | tf_op jit(solution)/shard_map/reduce_scatter | solution.py:172
  265.9 11.2 %reduce-scatter.7.cloned.1.call-start = ((), (), s32[]{:S(2)}) async-start(), calls=%async_computation.7 | async-start | bytes 3932160 | tf_op jit(solution)/shard_map/reduce_scatter | solution.py:196
  277.1 52.3 %all-gather.11.cloned.1.call-done = bf16[2048,768]{1,0:T(8,128)(2,1)} async-done(((bf16[512,768]{1,0:T(8,128)(2,1)}), bf16[2048,768]{1,0:T(8,128)(2,1)}) %all-gather.11.cloned.1.call-update) | async-done | bytes 3145744 | tf_op jit(solution)/shard_map/all_gather | solution.py:184
  329.5 11.0 %convert_reduce_fusion = (f32[768]{0:T(1024)}, bf16[2048,768]{1,0:T(8,128)(2,1)S(1)}) fusion(f32[2048,768]{1,0:T(8,128)} %get-tuple-element.89, f32[2048,768]{1,0:T(8,128)} %get-tuple-element.126, f32[768]{0:T(1024)} %convert_element_type.191, bf16[2048,768]{1,0:T(8,128)(2,1)} %all-gather.11.cloned.1.call-done, bf16[768,768]{1,0:T(8,128)(2,1)} %param.26), kind=kOutput, calls=%fused_computation.9 | convolution fusion | flops 2442657024 | bytes 20060160 | tf_op jit(solution)/shard_map/dot_general | solution.py:23
  342.2 4.0 convolution_convert_fusion
  346.3 5.7 fusion.60
  367.6 11.1 %collective-permute-done.5 = f32[192,768]{1,0:T(8,128)} collective-permute-done((f32[192,768]{1,0:T(8,128)}, f32[192,768]{1,0:T(8,128)}, u32[]{:S(2)}, u32[]{:S(2)}) %collective-permute-start.5) | collective-permute-done | bytes 589856 | tf_op jit(solution)/shard_map/ppermute | solution.py:83
  382.2 8.4 %collective-permute-done.2 = f32[192,768]{1,0:T(8,128)} collective-permute-done((f32[192,768]{1,0:T(8,128)}, f32[192,768]{1,0:T(8,128)}, u32[]{:S(2)}, u32[]{:S(2)}) %collective-permute-start.2) | collective-permute-done | bytes 589856 | tf_op jit(solution)/shard_map/ppermute | solution.py:83
  415.4 10.3 %multiply_reduce_fusion = (f32[12,512]{1,0:T(8,128)S(1)}, f32[12,512,512]{1,2,0:T(8,128)}) fusion(f32[12,512,512]{1,2,0:T(8,128)S(1)} %bitcast.136, f32[12,512]{1,0:T(8,128)S(1)} %copy-done.25, pred[512]{0:T(512)(128)(4,1)S(1)} %copy-done.40, bf16[512,12,64]{0,2,1:T(8,128)(2,1)S(1)} %bitcast.148, f32[512,12,64]{0,2,1:T(8,128)S(1)} %bitcast.140, ...), kind=kOutput, calls=%fused_computation.1 | convolution fusion | flops 419162112 | bytes 27577856 | tf_op jit(solution)/shard_map/pqhe,pkhe->phqk/dot_general | solution.py:46
  425.7 7.2 %multiply_convert_fusion = bf16[12,512,512]{1,2,0:T(8,128)(2,1)S(1)} fusion(f32[12,512,512]{1,2,0:T(8,128)} %get-tuple-element.128, f32[12,512,512]{1,2,0:T(8,128)S(1)} %bitcast.136, f32[12,512]{1,0:T(8,128)S(1)} %get-tuple-element.127, f32[12,512]{1,0:T(8,128)S(1)} %copy-done.25, pred[512]{0:T(512)(128)(4,1)S(1)} %copy-done.40), kind=kLoop, calls=%fused_computation | loop fusion | flops 18874368 | bytes 31506944 | tf_op jit(solution)/shard_map/convert_element_type | solution.py:50
  438.1 4.9 convolution_convert_fusion.2
  452.9 7.4 %collective-permute-done.8 = bf16[192,768]{1,0:T(8,128)(2,1)S(1)} collective-permute-done((bf16[192,768]{1,0:T(8,128)(2,1)S(1)}, bf16[192,768]{1,0:T(8,128)(2,1)S(1)}, u32[]{:S(2)}, u32[]{:S(2)}) %collective-permute-start.8) | collective-permute-done | bytes 294944 | tf_op jit(solution)/shard_map/ppermute | solution.py:83
  465.7 25.5 %reduce-scatter.9.cloned.1.call-done = bf16[288,768]{1,0:T(8,128)(2,1)} async-done(((bf16[2304,768]{1,0:T(8,128)(2,1)}), bf16[288,768]{1,0:T(8,128)(2,1)}) %reduce-scatter.9.cloned.1.call-update) | async-done | bytes 442384 | tf_op jit(solution)/shard_map/reduce_scatter | solution.py:258
  498.3 6.7 %collective-permute-done.14 = bf16[192,768]{1,0:T(8,128)(2,1)S(1)} collective-permute-done((bf16[192,768]{1,0:T(8,128)(2,1)S(1)}, bf16[192,768]{1,0:T(8,128)(2,1)S(1)}, u32[]{:S(2)}, u32[]{:S(2)}) %collective-permute-start.14) | collective-permute-done | bytes 294944 | tf_op jit(solution)/shard_map/ppermute | solution.py:98
  506.0 4.1 collective-permute-done.11
  515.0 14.5 %reduce-scatter.11.cloned.1.call-done = f32[1,416,192]{1,2,0:T(8,128)} async-done(((f32[4,416,192]{1,2,0:T(8,128)}), f32[1,416,192]{1,2,0:T(8,128)}) %reduce-scatter.11.cloned.1.call-update) | async-done | bytes 319504 | tf_op jit(solution)/shard_map/reduce_scatter | solution.py:265
  529.6 5.2 fusion.26
  534.8 27.7 %all-gather.15.cloned.1.call-done = f32[8,416,192]{1,2,0:T(8,128)} async-done(((f32[1,416,192]{1,2,0:T(8,128)}), f32[8,416,192]{1,2,0:T(8,128)}) %all-gather.15.cloned.1.call-update) | async-done | bytes 2555920 | tf_op jit(solution)/shard_map/all_gather | solution.py:279
  (285 shorter events, 139.3 us)
Async XLA Ops:
  7.2 61.1 %all-gather.13.cloned.1.call-start = ((), (), s32[]{:S(2)}) async-start(), calls=%async_computation.10 | async-start | bytes 3194880 | tf_op jit(solution)/shard_map/all_gather | solution.py:137
  11.3 163.5 %all-gather.9.cloned.1.call-start = ((), (), s32[]{:S(2)}) async-start(), calls=%async_computation.4 | async-start | bytes 3932160 | tf_op jit(solution)/shard_map/all_gather | solution.py:168
  68.3 5.2 collective-permute-start
  112.4 145.6 %reduce-scatter.5.cloned.1.call-start = ((), (), s32[]{:S(2)}) async-start(), calls=%async_computation.5 | async-start | bytes 3932160 | tf_op jit(solution)/shard_map/reduce_scatter | solution.py:172
  198.9 130.6 %all-gather.11.cloned.1.call-start = ((), (), s32[]{:S(2)}) async-start(), calls=%async_computation.6 | async-start | bytes 3932160 | tf_op jit(solution)/shard_map/all_gather | solution.py:184
  265.9 139.5 %reduce-scatter.7.cloned.1.call-start = ((), (), s32[]{:S(2)}) async-start(), calls=%async_computation.7 | async-start | bytes 3932160 | tf_op jit(solution)/shard_map/reduce_scatter | solution.py:196
  346.3 144.9 %reduce-scatter.9.cloned.1.call-start = ((), (), s32[]{:S(2)}) async-start(), calls=%async_computation.8 | async-start | bytes 3981312 | tf_op jit(solution)/shard_map/reduce_scatter | solution.py:258
  356.6 3.0 collective-permute-start.4
  356.6 7.1 %collective-permute-start.1 = (f32[384,768]{1,0:T(8,128)}, f32[384,768]{1,0:T(8,128)}, u32[]{:S(2)}, u32[]{:S(2)}) collective-permute-start(f32[384,768]{1,0:T(8,128)} %get-tuple-element.130), channel_id=1, source_target_pairs={{0,4},{4,0},{8,12},{12,8},{16,20},{20,16},{24,28},{28,24},{1,5},{5... | collective-permute-start | bytes 3538952 | tf_op jit(solution)/shard_map/ppermute | solution.py:83
  362.3 16.5 %collective-permute-start.5 = (f32[192,768]{1,0:T(8,128)}, f32[192,768]{1,0:T(8,128)}, u32[]{:S(2)}, u32[]{:S(2)}) collective-permute-start(f32[192,768]{1,0:T(8,128)} %constant_dynamic-slice_fusion.1), channel_id=1, source_target_pairs={{0,8},{4,12},{8,0},{12,4},{16,24},{20,28},{24,16},{28,20},{1,9},{5... | collective-permute-start | bytes 1769480 | tf_op jit(solution)/shard_map/ppermute | solution.py:83
  367.0 23.5 %collective-permute-start.2 = (f32[192,768]{1,0:T(8,128)}, f32[192,768]{1,0:T(8,128)}, u32[]{:S(2)}, u32[]{:S(2)}) collective-permute-start(f32[192,768]{1,0:T(8,128)} %constant_dynamic-slice_fusion.4), channel_id=1, source_target_pairs={{0,8},{4,12},{8,0},{12,4},{16,24},{20,28},{24,16},{28,20},{1,9},{5... | collective-permute-start | bytes 1769480 | tf_op jit(solution)/shard_map/ppermute | solution.py:83
  380.7 16.1 %collective-permute-start.6 = (f32[96,768]{1,0:T(8,128)}, f32[96,768]{1,0:T(8,128)}, u32[]{:S(2)}, u32[]{:S(2)}) collective-permute-start(f32[96,768]{1,0:T(8,128)} %constant_dynamic-slice_fusion), channel_id=1, source_target_pairs={{0,16},{4,20},{8,24},{12,28},{16,0},{20,4},{24,8},{28,12},{1,17},{... | collective-permute-start | bytes 884744 | tf_op jit(solution)/shard_map/ppermute | solution.py:83
  392.5 8.5 %collective-permute-start.3 = (f32[96,768]{1,0:T(8,128)}, f32[96,768]{1,0:T(8,128)}, u32[]{:S(2)}, u32[]{:S(2)}) collective-permute-start(f32[96,768]{1,0:T(8,128)} %constant_dynamic-slice_fusion.3), channel_id=1, source_target_pairs={{0,16},{4,20},{8,24},{12,28},{16,0},{20,4},{24,8},{28,12},{1,17},{... | collective-permute-start | bytes 884744 | tf_op jit(solution)/shard_map/ppermute | solution.py:83
  443.1 86.5 %reduce-scatter.11.cloned.1.call-start = ((), (), s32[]{:S(2)}) async-start(), calls=%async_computation.9 | async-start | bytes 1966080 | tf_op jit(solution)/shard_map/reduce_scatter | solution.py:265
  444.3 52.3 %collective-permute-start.10 = (bf16[96,768]{1,0:T(8,128)(2,1)}, bf16[96,768]{1,0:T(8,128)(2,1)}, u32[]{:S(2)}, u32[]{:S(2)}) collective-permute-start(bf16[96,768]{1,0:T(8,128)(2,1)} %dynamic-slice_add_fusion.5), channel_id=1, source_target_pairs={{0,16},{4,20},{8,24},{12,28},{16,0},{20,4},{24,8},{28,12},{1,17},{... | collective-permute-start | bytes 442376 | tf_op jit(solution)/shard_map/ppermute | solution.py:98
  445.8 48.2 %collective-permute-start.13 = (bf16[96,768]{1,0:T(8,128)(2,1)}, bf16[96,768]{1,0:T(8,128)(2,1)}, u32[]{:S(2)}, u32[]{:S(2)}) collective-permute-start(bf16[96,768]{1,0:T(8,128)(2,1)} %dynamic-slice_add_fusion.4), channel_id=1, source_target_pairs={{0,16},{4,20},{8,24},{12,28},{16,0},{20,4},{24,8},{28,12},{1,17},{... | collective-permute-start | bytes 442376 | tf_op jit(solution)/shard_map/ppermute | solution.py:98
  448.7 2.4 collective-permute-start.7
  451.2 9.1 %collective-permute-start.8 = (bf16[192,768]{1,0:T(8,128)(2,1)S(1)}, bf16[192,768]{1,0:T(8,128)(2,1)S(1)}, u32[]{:S(2)}, u32[]{:S(2)}) collective-permute-start(bf16[192,768]{1,0:T(8,128)(2,1)S(1)} %dynamic-slice_convert_fusion.1), channel_id=1, source_target_pairs={{0,8},{4,12},{8,0},{12,4},{16,24},{20,28},{24,16},{28,20},{1,9},{5... | collective-permute-start | bytes 884744 | tf_op jit(solution)/shard_map/ppermute | solution.py:83
  460.4 5.2 collective-permute-start.9
  494.0 68.5 %all-gather.15.cloned.1.call-start = ((), (), s32[]{:S(2)}) async-start(), calls=%async_computation.11 | async-start | bytes 3538944 | tf_op jit(solution)/shard_map/all_gather | solution.py:279
  495.1 9.9 %collective-permute-start.14 = (bf16[192,768]{1,0:T(8,128)(2,1)S(1)}, bf16[192,768]{1,0:T(8,128)(2,1)S(1)}, u32[]{:S(2)}, u32[]{:S(2)}) collective-permute-start(bf16[192,768]{1,0:T(8,128)(2,1)S(1)} %pad_maximum_fusion.6), channel_id=1, source_target_pairs={{0,8},{4,12},{8,0},{12,4},{16,24},{20,28},{24,16},{28,20},{1,9},{5... | collective-permute-start | bytes 884744 | tf_op jit(solution)/shard_map/ppermute | solution.py:98
  497.7 12.4 %collective-permute-start.11 = (bf16[192,768]{1,0:T(8,128)(2,1)S(1)}, bf16[192,768]{1,0:T(8,128)(2,1)S(1)}, u32[]{:S(2)}, u32[]{:S(2)}) collective-permute-start(bf16[192,768]{1,0:T(8,128)(2,1)S(1)} %pad_maximum_fusion.5), channel_id=1, source_target_pairs={{0,8},{4,12},{8,0},{12,4},{16,24},{20,28},{24,16},{28,20},{1,9},{5... | collective-permute-start | bytes 884744 | tf_op jit(solution)/shard_map/ppermute | solution.py:98
  506.0 5.0 collective-permute-start.15
  511.0 2.2 collective-permute-start.12
  (57 other events, 523.4 us)
Sparse Core Ops, SparseCore 0:
  11.4 56.8 all-gather.12
  112.6 62.2 all-gather.8
  199.0 59.0 reduce-scatter.4
  266.1 63.3 all-gather.10
  346.4 59.0 reduce-scatter.6
  443.2 47.9 reduce-scatter.8
  494.1 35.4 reduce-scatter.10
  531.5 31.0 all-gather.14
where the time goes:
time: 597 us; the launch traced here: 587 us
  waiting for transfers between devices  353 us (59%)
  matrix products  89.3 us (15%)
  other arithmetic  58.8 us (10%)
  local copies, waits for them, and re-layouts  46.3 us (8%)
  starting transfers between devices  24.3 us (4%)
  between operations  15.5 us (3%)
    all_gather x1, waiting for transfers between devices, per_device(): ffn_rows = lax.all_gather(middle_low, 'tensor', axis=0, tiled=True)  61 us
    reduce_scatter x1, waiting for transfers between devices, per_device(): lax.psum_scatter(jnp.dot(hidden, down_weight, preferred_element_type=jnp....  59.1 us
    all_gather x1, waiting for transfers between devices, per_device(): mine = lax.all_gather(mine, 'tensor', axis=0, tiled=False)  56.9 us
    all_gather x1, waiting for transfers between devices, per_device(): branch_rows = lax.all_gather(branch_grad, 'tensor', axis=0, tiled=True)  52.3 us
    ppermute x9, waiting for transfers between devices, dp_halve(): got = lax.ppermute(give, 'dp', [(i, i ^ 1 << step) for i in range(dp_size)])  37.6 us
    all_gather x1, waiting for transfers between devices, per_device(): joined = lax.all_gather(joined, 'dp', axis=0, tiled=False)  27.7 us
    dot_general x5, matrix products, contract(): lax.dot_general(left, right, (((left_dim,), (right_dim,)), ((), ())), pre...  25.7 us
    reduce_scatter x1, waiting for transfers between devices, per_device(): lax.psum_scatter(grad_qkv_full.reshape(3 * width, width).astype(jnp.bfloa...  25.5 us
  transfers between devices with their start and end apart: 24, of which 19 were waited for; matrix products, arithmetic and copies ran while one was open for 8% of the time, Pallas kernels for 0%

commit v1 on v0

--- a/solution.py
+++ b/solution.py
@@ -7,6 +7,25 @@
 LEN = 512
 EPS = 1e-12
 NEG = -1e30
+
+
+def watch_region(m, on_dim):
+    z1 = list(m.shape[1:])
+    z1[on_dim] *= m.shape[0]
+    v_now = jnp.moveaxis(m, 0, on_dim).reshape(z1)
+    return v_now
+
+
+def direct_ways(slab_in, which_axis):
+    block_out = slab_in[None]
+    amount_of = lax.axis_size(which_axis)
+    for kk in range(amount_of.bit_length() - 1):
+        x_now = 1 << kk
+        answer = lax.ppermute(block_out, which_axis, [(u, u ^ x_now) for u in range(amount_of)])
+        low = jnp.stack([block_out, answer])
+        lower = lax.axis_index(which_axis) >> kk & 1
+        block_out = jnp.where(lower == 0, low, low[::-1]).reshape(-1, *slab_in.shape)
+    return block_out
 
 
 def layer_norm(values, gain_vec, shift_vec):
@@ -165,7 +184,7 @@
             layer_norm, own_tokens + attn_out + out_bias, norm1_gain, norm1_shift
         )
         middle_low = middle.astype(jnp.bfloat16)
-        ffn_rows = lax.all_gather(middle_low, "tensor", axis=0, tiled=True)
+        ffn_rows = watch_region(direct_ways(middle_low, "tensor"), 0)
         pre_act = jnp.dot(ffn_rows, up_weight, preferred_element_type=jnp.float32) + up_bias
         activated, gelu_back = jax.vjp(gelu_exact, pre_act)
         hidden = activated.astype(jnp.bfloat16)

time: 597 us -> 633 us (1.060)
  waiting for transfers between devices: 353 us -> 380 us
  other arithmetic: 58.8 us -> 66.6 us
    ppermute x0 -> x2, waiting for transfers between devices: none -> 88.2 us  [direct_ways(): lax.ppermute(block_out, which_axis, [(u, u ^ x_now) for u in range(amount...]
    all_gather x1 -> x0, waiting for transfers between devices: 61 us -> none  [per_device(): ffn_rows = lax.all_gather(middle_low, 'tensor', axis=0, tiled=True)]
    unnamed x122 -> x124, local copies, waits for them, and re-layouts: 16.4 us -> 15.9 us
  transfers between devices with their start and end apart: 24 -> 25, of which waited for: 19 -> 20; matrix products, arithmetic and copies ran while one was open for 8% -> 8% of each run, Pallas kernels for 0% -> 0%
where the time goes in v1:
time: 633 us; the launch traced here: 622 us
  waiting for transfers between devices  380 us (60%)
  matrix products  89.3 us (14%)
  other arithmetic  66.6 us (11%)
  local copies, waits for them, and re-layouts  45.7 us (7%)
  starting transfers between devices  25.4 us (4%)
  between operations  15.5 us (2%)
    ppermute x2, waiting for transfers between devices, direct_ways(): lax.ppermute(block_out, which_axis, [(u, u ^ x_now) for u in range(amount...  88.2 us
    reduce_scatter x1, waiting for transfers between devices, per_device(): lax.psum_scatter(jnp.dot(hidden, down_weight, preferred_element_type=jnp....  59.2 us
    all_gather x1, waiting for transfers between devices, per_device(): mine = lax.all_gather(mine, 'tensor', axis=0, tiled=False)  56.9 us
    all_gather x1, waiting for transfers between devices, per_device(): branch_rows = lax.all_gather(branch_grad, 'tensor', axis=0, tiled=True)  52.3 us
    ppermute x9, waiting for transfers between devices, dp_halve(): got = lax.ppermute(give, 'dp', [(i, i ^ 1 << step) for i in range(dp_size)])  37.6 us
    all_gather x1, waiting for transfers between devices, per_device(): joined = lax.all_gather(joined, 'dp', axis=0, tiled=False)  27.7 us
    dot_general x5, matrix products, contract(): lax.dot_general(left, right, (((left_dim,), (right_dim,)), ((), ())), pre...  25.7 us
    reduce_scatter x1, waiting for transfers between devices, per_device(): lax.psum_scatter(grad_qkv_full.reshape(3 * width, width).astype(jnp.bfloa...  25.5 us
  transfers between devices with their start and end apart: 25, of which 20 were waited for; matrix products, arithmetic and copies ran while one was open for 8% of the time, Pallas kernels for 0%

profile of v1, /device:TPU:0, one launch (start us, length us, event | category | flops | bytes accessed | tf_op | source)
XLA Modules:
  0.0 622.3 jit_solution(9044541020246240394)
XLA Ops:
  11.3 56.9 %all-gather.10.cloned.1.call-done = bf16[4,1544,192]{1,2,0:T(8,128)(2,1)} async-done(((bf16[1,1544,192]{1,2,0:T(8,128)(2,1)}), bf16[4,1544,192]{1,2,0:T(8,128)(2,1)}) %all-gather.10.cloned.1.call-update) | async-done | bytes 2371600 | tf_op jit(solution)/shard_map/all_gather | solution.py:156
  83.8 5.0 fusion
  93.5 10.1 %fusion.1 = bf16[12,512,512]{1,2,0:T(8,128)(2,1)} fusion(f32[12,512,512]{1,2,0:T(8,128)} %copy-done.2, f32[12,512]{1,0:T(8,128)S(1)} %log_add_fusion, pred[512]{0:T(512)(128)(4,1)S(1)} %copy-done.39), kind=kLoop, calls=%fused_computation.7 | loop fusion | flops 12582912 | bytes 18899456 | tf_op jit(solution)/shard_map/convert_element_type | solution.py:57
  103.6 4.1 convolution_convert_fusion.5
  112.9 19.6 %collective-permute-done.1 = bf16[1,512,768]{2,1,0:T(8,128)(2,1)} collective-permute-done((bf16[1,512,768]{2,1,0:T(8,128)(2,1)}, bf16[1,512,768]{2,1,0:T(8,128)(2,1)}, u32[]{:S(2)}, u32[]{:S(2)}) %collective-permute-start.1) | collective-permute-done | bytes 786464 | tf_op jit(solution)/shard_map/ppermute | solution.py:24
  137.7 68.6 %collective-permute-done.2 = bf16[2,512,768]{2,1,0:T(8,128)(2,1)} collective-permute-done((bf16[2,512,768]{2,1,0:T(8,128)(2,1)}, bf16[2,512,768]{2,1,0:T(8,128)(2,1)}, u32[]{:S(2)}, u32[]{:S(2)}) %collective-permute-start.2) | collective-permute-done | bytes 1572896 | tf_op jit(solution)/shard_map/ppermute | solution.py:24
  209.1 18.4 %multiply_convert_fusion.1 = (bf16[2048,768]{1,0:T(8,128)(2,1)S(1)}, f32[2048,768]{1,0:T(8,128)}, f32[2048,768]{1,0:T(8,128)}) fusion(f32[768]{0:T(1024)S(1)} %convert_element_type.191, bf16[2048,768]{1,0:T(8,128)(2,1)S(1)} %bitcast.169, bf16[768,768]{1,0:T(8,128)(2,1)S(1)} %copy-done), kind=kOutput, calls=%fused_computation.11 | convolution fusion | flops 2519728128 | bytes 20057088 | tf_op jit(solution)/shard_map/dot_general | solution.py:188
  233.2 59.2 %reduce-scatter.5.cloned.1.call-done = bf16[512,768]{1,0:T(8,128)(2,1)} async-done(((bf16[2048,768]{1,0:T(8,128)(2,1)}), bf16[512,768]{1,0:T(8,128)(2,1)}) %reduce-scatter.5.cloned.1.call-update) | async-done | bytes 786448 | tf_op jit(solution)/shard_map/reduce_scatter | solution.py:191
  301.1 11.2 %reduce-scatter.7.cloned.1.call-start = ((), (), s32[]{:S(2)}) async-start(), calls=%async_computation.6 | async-start | bytes 3932160 | tf_op jit(solution)/shard_map/reduce_scatter | solution.py:215
  312.3 52.3 %all-gather.8.cloned.1.call-done = bf16[2048,768]{1,0:T(8,128)(2,1)} async-done(((bf16[512,768]{1,0:T(8,128)(2,1)}), bf16[2048,768]{1,0:T(8,128)(2,1)}) %all-gather.8.cloned.1.call-update) | async-done | bytes 3145744 | tf_op jit(solution)/shard_map/all_gather | solution.py:203
  364.6 11.0 %convert_reduce_fusion = (f32[768]{0:T(1024)}, bf16[2048,768]{1,0:T(8,128)(2,1)S(1)}) fusion(f32[2048,768]{1,0:T(8,128)} %get-tuple-element.89, f32[2048,768]{1,0:T(8,128)} %get-tuple-element.128, f32[768]{0:T(1024)} %copy-done.42, bf16[2048,768]{1,0:T(8,128)(2,1)} %all-gather.8.cloned.1.call-done, bf16[768,768]{1,0:T(8,128)(2,1)} %param.26), kind=kOutput, calls=%fused_computation.9 | convolution fusion | flops 2442657024 | bytes 20060160 | tf_op jit(solution)/shard_map/dot_general | solution.py:42
  381.5 5.7 fusion.61
  402.8 11.1 %collective-permute-done.7 = f32[192,768]{1,0:T(8,128)} collective-permute-done((f32[192,768]{1,0:T(8,128)}, f32[192,768]{1,0:T(8,128)}, u32[]{:S(2)}, u32[]{:S(2)}) %collective-permute-start.7) | collective-permute-done | bytes 589856 | tf_op jit(solution)/shard_map/ppermute | solution.py:102
  417.3 8.4 %collective-permute-done.4 = f32[192,768]{1,0:T(8,128)} collective-permute-done((f32[192,768]{1,0:T(8,128)}, f32[192,768]{1,0:T(8,128)}, u32[]{:S(2)}, u32[]{:S(2)}) %collective-permute-start.4) | collective-permute-done | bytes 589856 | tf_op jit(solution)/shard_map/ppermute | solution.py:102
  450.6 10.3 %multiply_reduce_fusion = (f32[12,512]{1,0:T(8,128)S(1)}, f32[12,512,512]{1,2,0:T(8,128)}) fusion(f32[12,512,512]{1,2,0:T(8,128)S(1)} %bitcast.147, f32[12,512]{1,0:T(8,128)S(1)} %copy-done.26, pred[512]{0:T(512)(128)(4,1)S(1)} %copy-done.40, bf16[512,12,64]{0,2,1:T(8,128)(2,1)S(1)} %bitcast.159, f32[512,12,64]{0,2,1:T(8,128)S(1)} %bitcast.151, ...), kind=kOutput, calls=%fused_computation.1 | convolution fusion | flops 419162112 | bytes 27577856 | tf_op jit(solution)/shard_map/pqhe,pkhe->phqk/dot_general | solution.py:65
  460.9 7.2 %multiply_convert_fusion = bf16[12,512,512]{1,2,0:T(8,128)(2,1)S(1)} fusion(f32[12,512,512]{1,2,0:T(8,128)} %get-tuple-element.130, f32[12,512,512]{1,2,0:T(8,128)S(1)} %bitcast.147, f32[12,512]{1,0:T(8,128)S(1)} %get-tuple-element.129, f32[12,512]{1,0:T(8,128)S(1)} %copy-done.26, pred[512]{0:T(512)(128)(4,1)S(1)} %copy-done.40), kind=kLoop, calls=%fused_computation | loop fusion | flops 18874368 | bytes 31506944 | tf_op jit(solution)/shard_map/convert_element_type | solution.py:69
  473.4 4.9 convolution_convert_fusion.2
  488.1 7.5 %collective-permute-done.10 = bf16[192,768]{1,0:T(8,128)(2,1)S(1)} collective-permute-done((bf16[192,768]{1,0:T(8,128)(2,1)S(1)}, bf16[192,768]{1,0:T(8,128)(2,1)S(1)}, u32[]{:S(2)}, u32[]{:S(2)}) %collective-permute-start.10) | collective-permute-done | bytes 294944 | tf_op jit(solution)/shard_map/ppermute | solution.py:102
  500.9 25.5 %reduce-scatter.9.cloned.1.call-done = bf16[288,768]{1,0:T(8,128)(2,1)} async-done(((bf16[2304,768]{1,0:T(8,128)(2,1)}), bf16[288,768]{1,0:T(8,128)(2,1)}) %reduce-scatter.9.cloned.1.call-update) | async-done | bytes 442384 | tf_op jit(solution)/shard_map/reduce_scatter | solution.py:277
  533.6 6.7 %collective-permute-done.16 = bf16[192,768]{1,0:T(8,128)(2,1)S(1)} collective-permute-done((bf16[192,768]{1,0:T(8,128)(2,1)S(1)}, bf16[192,768]{1,0:T(8,128)(2,1)S(1)}, u32[]{:S(2)}, u32[]{:S(2)}) %collective-permute-start.16) | collective-permute-done | bytes 294944 | tf_op jit(solution)/shard_map/ppermute | solution.py:117
  541.3 4.1 collective-permute-done.13
  550.3 14.5 %reduce-scatter.11.cloned.1.call-done = f32[1,416,192]{1,2,0:T(8,128)} async-done(((f32[4,416,192]{1,2,0:T(8,128)}), f32[1,416,192]{1,2,0:T(8,128)}) %reduce-scatter.11.cloned.1.call-update) | async-done | bytes 319504 | tf_op jit(solution)/shard_map/reduce_scatter | solution.py:284
  564.9 5.2 fusion.26
  570.1 27.7 %all-gather.12.cloned.1.call-done = f32[8,416,192]{1,2,0:T(8,128)} async-done(((f32[1,416,192]{1,2,0:T(8,128)}), f32[8,416,192]{1,2,0:T(8,128)}) %all-gather.12.cloned.1.call-update) | async-done | bytes 2555920 | tf_op jit(solution)/shard_map/all_gather | solution.py:298
  (293 shorter events, 151.3 us)
Async XLA Ops:
  7.2 61.1 %all-gather.10.cloned.1.call-start = ((), (), s32[]{:S(2)}) async-start(), calls=%async_computation.9 | async-start | bytes 3194880 | tf_op jit(solution)/shard_map/all_gather | solution.py:156
  11.3 281.1 %reduce-scatter.5.cloned.1.call-start = ((), (), s32[]{:S(2)}) async-start(), calls=%async_computation.4 | async-start | bytes 3932160 | tf_op jit(solution)/shard_map/reduce_scatter | solution.py:191
  68.3 5.2 collective-permute-start
  112.6 19.9 %collective-permute-start.1 = (bf16[1,512,768]{2,1,0:T(8,128)(2,1)}, bf16[1,512,768]{2,1,0:T(8,128)(2,1)}, u32[]{:S(2)}, u32[]{:S(2)}) collective-permute-start(bf16[1,512,768]{2,1,0:T(8,128)(2,1)} %fusion.90), channel_id=1, source_target_pairs={{0,1},{1,0},{2,3},{3,2},{4,5},{5,4},{6,7},{7,6},{8,9},{9,8},{10,11... | collective-permute-start | bytes 2359304 | tf_op jit(solution)/shard_map/ppermute | solution.py:24
  135.8 70.5 %collective-permute-start.2 = (bf16[2,512,768]{2,1,0:T(8,128)(2,1)}, bf16[2,512,768]{2,1,0:T(8,128)(2,1)}, u32[]{:S(2)}, u32[]{:S(2)}) collective-permute-start(bf16[2,512,768]{2,1,0:T(8,128)(2,1)} %get-tuple-element.104), channel_id=1, source_target_pairs={{0,2},{1,3},{2,0},{3,1},{4,6},{5,7},{6,4},{7,5},{8,10},{9,11},{10,... | collective-permute-start | bytes 4718600 | tf_op jit(solution)/shard_map/ppermute | solution.py:24
  233.2 131.4 %all-gather.8.cloned.1.call-start = ((), (), s32[]{:S(2)}) async-start(), calls=%async_computation.5 | async-start | bytes 3932160 | tf_op jit(solution)/shard_map/all_gather | solution.py:203
  301.1 139.5 %reduce-scatter.7.cloned.1.call-start = ((), (), s32[]{:S(2)}) async-start(), calls=%async_computation.6 | async-start | bytes 3932160 | tf_op jit(solution)/shard_map/reduce_scatter | solution.py:215
  381.4 145.1 %reduce-scatter.9.cloned.1.call-start = ((), (), s32[]{:S(2)}) async-start(), calls=%async_computation.7 | async-start | bytes 3981312 | tf_op jit(solution)/shard_map/reduce_scatter | solution.py:277
  391.8 3.0 collective-permute-start.6
  391.8 7.1 %collective-permute-start.3 = (f32[384,768]{1,0:T(8,128)}, f32[384,768]{1,0:T(8,128)}, u32[]{:S(2)}, u32[]{:S(2)}) collective-permute-start(f32[384,768]{1,0:T(8,128)} %get-tuple-element.132), channel_id=1, source_target_pairs={{0,4},{4,0},{8,12},{12,8},{16,20},{20,16},{24,28},{28,24},{1,5},{5... | collective-permute-start | bytes 3538952 | tf_op jit(solution)/shard_map/ppermute | solution.py:102
  397.4 16.5 %collective-permute-start.7 = (f32[192,768]{1,0:T(8,128)}, f32[192,768]{1,0:T(8,128)}, u32[]{:S(2)}, u32[]{:S(2)}) collective-permute-start(f32[192,768]{1,0:T(8,128)} %constant_dynamic-slice_fusion.1), channel_id=1, source_target_pairs={{0,8},{4,12},{8,0},{12,4},{16,24},{20,28},{24,16},{28,20},{1,9},{5... | collective-permute-start | bytes 1769480 | tf_op jit(solution)/shard_map/ppermute | solution.py:102
  402.2 23.5 %collective-permute-start.4 = (f32[192,768]{1,0:T(8,128)}, f32[192,768]{1,0:T(8,128)}, u32[]{:S(2)}, u32[]{:S(2)}) collective-permute-start(f32[192,768]{1,0:T(8,128)} %constant_dynamic-slice_fusion.4), channel_id=1, source_target_pairs={{0,8},{4,12},{8,0},{12,4},{16,24},{20,28},{24,16},{28,20},{1,9},{5... | collective-permute-start | bytes 1769480 | tf_op jit(solution)/shard_map/ppermute | solution.py:102
  415.9 16.1 %collective-permute-start.8 = (f32[96,768]{1,0:T(8,128)}, f32[96,768]{1,0:T(8,128)}, u32[]{:S(2)}, u32[]{:S(2)}) collective-permute-start(f32[96,768]{1,0:T(8,128)} %constant_dynamic-slice_fusion), channel_id=1, source_target_pairs={{0,16},{4,20},{8,24},{12,28},{16,0},{20,4},{24,8},{28,12},{1,17},{... | collective-permute-start | bytes 884744 | tf_op jit(solution)/shard_map/ppermute | solution.py:102
  427.6 8.5 %collective-permute-start.5 = (f32[96,768]{1,0:T(8,128)}, f32[96,768]{1,0:T(8,128)}, u32[]{:S(2)}, u32[]{:S(2)}) collective-permute-start(f32[96,768]{1,0:T(8,128)} %constant_dynamic-slice_fusion.3), channel_id=1, source_target_pairs={{0,16},{4,20},{8,24},{12,28},{16,0},{20,4},{24,8},{28,12},{1,17},{... | collective-permute-start | bytes 884744 | tf_op jit(solution)/shard_map/ppermute | solution.py:102
  478.3 86.5 %reduce-scatter.11.cloned.1.call-start = ((), (), s32[]{:S(2)}) async-start(), calls=%async_computation.8 | async-start | bytes 1966080 | tf_op jit(solution)/shard_map/reduce_scatter | solution.py:284
  479.6 52.3 %collective-permute-start.12 = (bf16[96,768]{1,0:T(8,128)(2,1)}, bf16[96,768]{1,0:T(8,128)(2,1)}, u32[]{:S(2)}, u32[]{:S(2)}) collective-permute-start(bf16[96,768]{1,0:T(8,128)(2,1)} %dynamic-slice_add_fusion.5), channel_id=1, source_target_pairs={{0,16},{4,20},{8,24},{12,28},{16,0},{20,4},{24,8},{28,12},{1,17},{... | collective-permute-start | bytes 442376 | tf_op jit(solution)/shard_map/ppermute | solution.py:117
  481.0 48.3 %collective-permute-start.15 = (bf16[96,768]{1,0:T(8,128)(2,1)}, bf16[96,768]{1,0:T(8,128)(2,1)}, u32[]{:S(2)}, u32[]{:S(2)}) collective-permute-start(bf16[96,768]{1,0:T(8,128)(2,1)} %dynamic-slice_add_fusion.4), channel_id=1, source_target_pairs={{0,16},{4,20},{8,24},{12,28},{16,0},{20,4},{24,8},{28,12},{1,17},{... | collective-permute-start | bytes 442376 | tf_op jit(solution)/shard_map/ppermute | solution.py:117
  483.9 2.4 collective-permute-start.9
  486.5 9.1 %collective-permute-start.10 = (bf16[192,768]{1,0:T(8,128)(2,1)S(1)}, bf16[192,768]{1,0:T(8,128)(2,1)S(1)}, u32[]{:S(2)}, u32[]{:S(2)}) collective-permute-start(bf16[192,768]{1,0:T(8,128)(2,1)S(1)} %dynamic-slice_convert_fusion.1), channel_id=1, source_target_pairs={{0,8},{4,12},{8,0},{12,4},{16,24},{20,28},{24,16},{28,20},{1,9},{5... | collective-permute-start | bytes 884744 | tf_op jit(solution)/shard_map/ppermute | solution.py:102
  495.7 5.2 collective-permute-start.11
  529.3 68.5 %all-gather.12.cloned.1.call-start = ((), (), s32[]{:S(2)}) async-start(), calls=%async_computation.10 | async-start | bytes 3538944 | tf_op jit(solution)/shard_map/all_gather | solution.py:298
  530.4 9.9 %collective-permute-start.16 = (bf16[192,768]{1,0:T(8,128)(2,1)S(1)}, bf16[192,768]{1,0:T(8,128)(2,1)S(1)}, u32[]{:S(2)}, u32[]{:S(2)}) collective-permute-start(bf16[192,768]{1,0:T(8,128)(2,1)S(1)} %pad_maximum_fusion.8), channel_id=1, source_target_pairs={{0,8},{4,12},{8,0},{12,4},{16,24},{20,28},{24,16},{28,20},{1,9},{5... | collective-permute-start | bytes 884744 | tf_op jit(solution)/shard_map/ppermute | solution.py:117
  532.9 12.4 %collective-permute-start.13 = (bf16[192,768]{1,0:T(8,128)(2,1)S(1)}, bf16[192,768]{1,0:T(8,128)(2,1)S(1)}, u32[]{:S(2)}, u32[]{:S(2)}) collective-permute-start(bf16[192,768]{1,0:T(8,128)(2,1)S(1)} %pad_maximum_fusion.7), channel_id=1, source_target_pairs={{0,8},{4,12},{8,0},{12,4},{16,24},{20,28},{24,16},{28,20},{1,9},{5... | collective-permute-start | bytes 884744 | tf_op jit(solution)/shard_map/ppermute | solution.py:117
  541.3 5.0 collective-permute-start.17
  (59 other events, 642.7 us)
Sparse Core Ops, SparseCore 0:
  11.4 56.8 all-gather.9
  233.3 59.0 reduce-scatter.4
  301.2 63.3 all-gather.7
  381.5 59.0 reduce-scatter.6
  478.5 47.9 reduce-scatter.8
  529.4 35.4 reduce-scatter.10
  566.7 31.0 all-gather.11
